TPU v7x, 256 devices: a whole 4x4x8 slice. The times are simulated.
256 devices in a mesh: seq: 16 (over z, y_lo), chan: 16 (over y_hi, x, core).
Axes of the slice: x: 4, y: 4 (y_hi: 2, y_lo: 2; y = y_hi * 2 + y_lo), z: 8, core: 2. Of those that a mesh axis runs over, the one named last changes fastest.
Arguments:
- tokens: bfloat16 [4096, 4096], P('seq', 'chan'), may hold values from -6 to 6
- in_weight: bfloat16 [4096, 3, 4096], P(None, None, 'chan'), may hold values from -0.09375 to 0.09375
- short_weight: float32 [3, 3, 4096], P(None, None, 'chan'), may hold values from -3 to 3
- filter_taps: bfloat16 [4096, 4096], P(None, 'chan'), may hold values from -0.09375 to 0.09375
- cotangent: bfloat16 [4096, 4096], P('seq', 'chan'), may hold values from -1.5 to 1.5
Outputs:
- operator_out: bfloat16 [4096, 4096], P('seq', 'chan')
- stream_grads: bfloat16 [4096, 3, 4096], P('seq', None, 'chan')
- tap_grads: float32 [4096, 4096], P('seq', 'chan')
All inputs are finite; a program needn't handle non-finite values.
Results may differ from a plain program's by a relative error of at most 0.015.
Values may be sent and summed in bfloat16 or wider, within the bound.
No kernel may reach another device: no remote copies, remote signals or barrier semaphores. Data moves between devices by JAX's collectives and lax.ppermute only.
A program may use at most 128 MiB of HBM per device.

v0:
```python
import math
import jax
import jax.numpy as jnp
from jax import lax
from jax.sharding import PartitionSpec as P


def passed_along(block, axis, distance):
    devices = range(lax.axis_size(axis))
    route = [(i - distance, i) for i in devices if i - distance in devices]
    return lax.ppermute(block, axis, route)


def dft_tables(row_count):
    length = 2 * row_count
    sample = jnp.arange(length, dtype=jnp.int32)
    frequency = jnp.arange(row_count, dtype=jnp.int32)
    angles = (frequency[:, None] * sample[None, :] % length).astype(jnp.float32) * (
        2.0 * math.pi / length
    )
    parity = 1.0 - 2.0 * (sample % 2).astype(jnp.float32)
    lower_rows = jnp.where(frequency[:, None] == 0, parity[None, :], -jnp.sin(angles))
    forward = jnp.concatenate([jnp.cos(angles), lower_rows], axis=0)
    out_index = row_count + frequency
    back_angles = (out_index[:, None] * frequency[None, :] % length).astype(jnp.float32) * (
        2.0 * math.pi / length
    )
    factor = jnp.where(frequency == 0, 1.0, 2.0) / length
    out_parity = 1.0 - 2.0 * (out_index % 2).astype(jnp.float32)
    real_part = jnp.cos(back_angles) * factor[None, :]
    imag_part = jnp.where(
        frequency[None, :] == 0, out_parity[:, None] / length, -2.0 * jnp.sin(back_angles) / length
    )
    inverse = jnp.concatenate([real_part, imag_part], axis=1)
    return (forward, inverse)


def spectral_product(left_spec, right_spec):
    half_len = left_spec.shape[0] // 2
    left_spec = left_spec.astype(jnp.float32)
    right_spec = right_spec.astype(jnp.float32)
    left_re, left_im = (left_spec[:half_len], left_spec[half_len:])
    right_re, right_im = (right_spec[:half_len], right_spec[half_len:])
    first_row = (jnp.arange(half_len) == 0).reshape((half_len,) + (1,) * (left_spec.ndim - 1))
    cross_term = left_im * right_im
    real_out = left_re * right_re - jnp.where(first_row, 0.0, cross_term)
    imag_out = jnp.where(first_row, cross_term, left_re * right_im + left_im * right_re)
    return jnp.concatenate([real_out, imag_out], axis=0)


def spectral_adjoint(left_spec, grad_spec):
    half_len = left_spec.shape[0] // 2
    left_spec = left_spec.astype(jnp.float32)
    grad_spec = grad_spec.astype(jnp.float32)
    left_re, left_im = (left_spec[:half_len], left_spec[half_len:])
    grad_re, grad_im = (grad_spec[:half_len], grad_spec[half_len:])
    first_row = (jnp.arange(half_len) == 0).reshape((half_len,) + (1,) * (left_spec.ndim - 1))
    cross_term = left_im * grad_im
    real_out = left_re * grad_re + jnp.where(first_row, 0.0, cross_term)
    imag_out = jnp.where(first_row, cross_term, left_re * grad_im - left_im * grad_re)
    return jnp.concatenate([real_out, imag_out], axis=0)


def neighbour_rows(edge_rows, offset):
    return passed_along(edge_rows, "seq", offset)


def on_device(tokens, in_weight, short_weight, filter_taps, cotangent):
    row_count, local_width = tokens.shape
    spec_rows = 2 * row_count
    seq_count = lax.axis_size("seq")
    own_block = lax.axis_index("seq")
    forward, inverse = dft_tables(row_count)
    full_table = forward.astype(jnp.bfloat16)
    half_table = full_table[:, :row_count]
    back_table = inverse.astype(jnp.bfloat16)
    weight_cols = in_weight.reshape(in_weight.shape[0], 3 * local_width)
    streams = jnp.dot(
        lax.all_gather(tokens, "chan", axis=1, tiled=True),
        weight_cols,
        preferred_element_type=jnp.float32,
    )
    streams = streams.astype(jnp.bfloat16)
    before = neighbour_rows(streams[row_count - 2 :], 1)
    extended = (
        jnp.concatenate([before, streams], axis=0)
        .astype(jnp.float32)
        .reshape(row_count + 2, 3, local_width)
    )
    conv_out = (
        short_weight[:, 0] * extended[2:]
        + short_weight[:, 1] * extended[1:-1]
        + short_weight[:, 2] * extended[:-2]
    )
    query_conv, key_conv, value_conv = (conv_out[:, 0], conv_out[:, 1], conv_out[:, 2])
    gated = (key_conv * value_conv).astype(jnp.bfloat16)
    own_spec = jnp.dot(half_table, gated, preferred_element_type=jnp.float32).astype(jnp.bfloat16)
    tap_blocks = filter_taps.reshape(seq_count, row_count, local_width)
    earlier = jnp.concatenate(
        [jnp.zeros((1, row_count, local_width), jnp.bfloat16), tap_blocks[:-1]], axis=0
    )
    segments = jnp.concatenate([earlier, tap_blocks], axis=1)
    filters = jnp.einsum(
        "fn,bnc->bfc", full_table, segments, preferred_element_type=jnp.float32
    ).astype(jnp.bfloat16)
    pieces = lax.all_gather(own_spec, "seq", axis=0, tiled=True)

    def forward_add_block(position, carried):
        lag_index = own_block - position
        incoming = lax.dynamic_slice_in_dim(pieces, position * spec_rows, spec_rows, 0)
        filter_spec = lax.dynamic_index_in_dim(
            filters, jnp.clip(lag_index, 0, seq_count - 1), 0, keepdims=False
        )
        return carried + jnp.where(lag_index >= 0, spectral_product(filter_spec, incoming), 0.0)

    mixed_spec = lax.fori_loop(
        0,
        pieces.shape[0] // spec_rows,
        forward_add_block,
        jnp.zeros((spec_rows, local_width), jnp.float32),
    )
    long_out = jnp.dot(
        back_table, mixed_spec.astype(jnp.bfloat16), preferred_element_type=jnp.float32
    ).astype(jnp.bfloat16)
    operator_out = (query_conv * long_out.astype(jnp.float32)).astype(jnp.bfloat16)
    cot_wide = cotangent.astype(jnp.float32)
    grad_long = (cot_wide * query_conv).astype(jnp.bfloat16)
    grad_query = cot_wide * long_out.astype(jnp.float32)
    grad_spec = jnp.dot(back_table.T, grad_long, preferred_element_type=jnp.float32).astype(
        jnp.bfloat16
    )
    start_state = (
        jnp.zeros((spec_rows, local_width), jnp.float32),
        jnp.zeros((seq_count, spec_rows, local_width), jnp.float32),
    )
    backward_pieces = lax.all_gather(grad_spec, "seq", axis=0, tiled=True)

    def backward_add_block(position, state):
        spectral_grad, filter_grad = state
        lag_index = position - own_block
        usable = lag_index >= 0
        clipped = jnp.clip(lag_index, 0, seq_count - 1)
        incoming = lax.dynamic_slice_in_dim(backward_pieces, position * spec_rows, spec_rows, 0)
        filter_spec = lax.dynamic_index_in_dim(filters, clipped, 0, keepdims=False)
        spectral_grad = spectral_grad + jnp.where(
            usable, spectral_adjoint(filter_spec, incoming), 0.0
        )
        current = lax.dynamic_index_in_dim(filter_grad, clipped, 0, keepdims=False)
        current = current + jnp.where(usable, spectral_adjoint(own_spec, incoming), 0.0)
        filter_grad = lax.dynamic_update_index_in_dim(filter_grad, current, clipped, 0)
        return (spectral_grad, filter_grad)

    spectral_grad, filter_grad = lax.fori_loop(
        0, backward_pieces.shape[0] // spec_rows, backward_add_block, start_state
    )
    grad_gated = jnp.dot(
        half_table.T, spectral_grad.astype(jnp.bfloat16), preferred_element_type=jnp.float32
    ).astype(jnp.bfloat16)
    tap_spec = jnp.einsum("fn,bfc->bnc", forward, filter_grad, precision=lax.Precision.HIGHEST)
    tap_terms = tap_spec[:, row_count:] + jnp.concatenate(
        [tap_spec[1:, :row_count], jnp.zeros((1, row_count, local_width), jnp.float32)], axis=0
    )
    tap_grads = lax.psum_scatter(
        tap_terms.reshape(seq_count * row_count, local_width).astype(jnp.bfloat16),
        "seq",
        scatter_dimension=0,
        tiled=True,
    ).astype(jnp.float32)
    gated_wide = grad_gated.astype(jnp.float32)
    grad_streams = jnp.stack(
        [grad_query, gated_wide * value_conv, gated_wide * key_conv], axis=1
    ).astype(jnp.bfloat16)
    grad_streams = grad_streams.reshape(row_count, 3 * local_width)
    after = neighbour_rows(grad_streams[:2], -1)
    padded = (
        jnp.concatenate([grad_streams, after], axis=0)
        .astype(jnp.float32)
        .reshape(row_count + 2, 3, local_width)
    )
    stream_grads = (
        short_weight[:, 0] * padded[:row_count]
        + short_weight[:, 1] * padded[1 : row_count + 1]
        + short_weight[:, 2] * padded[2:]
    ).astype(jnp.bfloat16)
    return (operator_out, stream_grads, tap_grads)


def solution(mesh):
    return jax.shard_map(
        on_device,
        mesh=mesh,
        in_specs=(
            P("seq", "chan"),
            P(None, None, "chan"),
            P(None, None, "chan"),
            P(None, "chan"),
            P("seq", "chan"),
        ),
        out_specs=(P("seq", "chan"), P("seq", None, "chan"), P("seq", "chan")),
        check_vma=False,
    )
```

profile of v0, /device:TPU:20, one launch (start us, length us, event | category | flops | bytes accessed | tf_op | source)
XLA Modules:
  0.0 376.9 jit_solution(4375459504469983553)
XLA Ops:
  8.0 8.7 %copy.31 = bf16[4096,3,256]{0,2,1:T(8,128)(2,1)} copy(bf16[4096,3,256]{2,0,1:T(8,128)(2,1)} %param.10) | data formatting | bytes 12582912 | tf_op args[1]
  18.9 44.9 %all-gather.4.cloned.1.call-done = bf16[256,4096]{1,0:T(8,128)(2,1)} async-done(((bf16[256,256]{1,0:T(8,128)(2,1)}), bf16[256,4096]{1,0:T(8,128)(2,1)}) %all-gather.4.cloned.1.call-update) | async-done | bytes 2097168 | tf_op jit(solution)/shard_map/all_gather | solution.py:79
  63.8 5.2 %convolution_convert_fusion = bf16[256,768]{1,0:T(8,128)(2,1)S(1)} fusion(bf16[256,4096]{1,0:T(8,128)(2,1)} %all-gather.4.cloned.1.call-done, bf16[4096,768]{0,1:T(8,128)(2,1)} %bitcast.104), kind=kOutput, calls=%fused_computation.38 | convolution fusion | flops 1610809344 | bytes 8781824 | tf_op jit(solution)/shard_map/dot_general | solution.py:78
  69.0 4.0 %collective-permute-start = (bf16[2,768]{1,0:T(2,128)(2,1)S(1)}, bf16[2,768]{1,0:T(2,128)(2,1)S(1)}, u32[]{:S(2)}, u32[]{:S(2)}) collective-permute-start(bf16[2,768]{1,0:T(2,128)(2,1)S(1)} %slice.215), channel_id=1, source_target_pairs={{0,16},{16,32},{32,48},{48,64},{64,80},{80,96},{96,112},{112,128},... | collective-permute-start | bytes 9224 | tf_op jit(solution)/shard_map/ppermute | solution.py:11
  82.0 2.3 copy.38
  84.3 3.9 %copy.39 = bf16[16,256,256]{1,2,0:T(8,128)(2,1)} copy(bf16[16,256,256]{2,1,0:T(8,128)(2,1)} %bitcast.102) | data formatting | bytes 4194304 | tf_op jit(solution)/shard_map/reshape | solution.py:98
  88.2 2.1 negate_select_fusion.2
  90.4 6.7 %convert_bitcast_fusion = bf16[16,512,256]{1,2,0:T(8,128)(2,1)} fusion(bf16[15,256,256]{1,2,0:T(8,128)(2,1)} %copy.38, bf16[16,256,256]{1,2,0:T(8,128)(2,1)} %copy.39, bf16[512,512]{1,0:T(8,128)(2,1)S(1)} %fusion.20), kind=kOutput, calls=%fused_computation.35 | convolution fusion | flops 2162163712 | bytes 8781824 | tf_op jit(solution)/shard_map/fn,bnc->bfc/dot_general | solution.py:103
  97.1 6.4 %copy.40 = bf16[16,512,256]{2,1,0:T(8,128)(2,1)} copy(bf16[16,512,256]{1,2,0:T(8,128)(2,1)} %convert_bitcast_fusion) | data formatting | bytes 8388608
  103.5 2.0 convolution_convert_fusion.2
  105.7 79.7 %all-gather.8.cloned.1.call-done = bf16[8192,256]{1,0:T(8,128)(2,1)} async-done(((bf16[512,256]{1,0:T(8,128)(2,1)}), bf16[8192,256]{1,0:T(8,128)(2,1)}) %all-gather.8.cloned.1.call-update) | async-done | bytes 4194320 | tf_op jit(solution)/shard_map/all_gather | solution.py:136
  185.4 4.2 %broadcast_in_dim.154 = f32[16,512,256]{2,1,0:T(8,128)} broadcast(f32[]{:T(128)} %constant.182.clone.1), dimensions={} | broadcast | bytes 8388612 | tf_op jit(solution)/shard_map/broadcast_in_dim | solution.py:134
  189.6 69.7 %while.31 = (s32[]{:T(128)}, f32[512,256]{1,0:T(8,128)S(1)}, f32[16,512,256]{2,1,0:T(8,128)}, s32[]{:T(128)}, bf16[16,512,256]{2,1,0:T(8,128)(2,1)}, /*index=5*/...) while((s32[]{:T(128)}, f32[512,256]{1,0:T(8,128)S(1)}, ...), condition=%wide.region_3.4_spmd.clone, body=%wide.region_2.3_spmd.clone.sunk | while | flops 2359563 | bytes 8127216 | solution.py:153
  196.4 1.9 fusion.74
  226.8 1.9 fusion.74
  231.2 1.9 fusion.74
  253.0 1.9 fusion.74
  257.3 2.0 fusion.74
  259.3 16.5 %convolution_bitcast_fusion = f32[16,512,256]{1,2,0:T(8,128)S(1)} fusion(f32[16,512,256]{2,1,0:T(8,128)} %get-tuple-element.224, f32[256,512]{1,0:T(8,128)S(1)} %get-tuple-element.350, f32[256,512]{1,0:T(8,128)S(1)} %get-tuple-element.351), kind=kOutput, calls=%fused_computation.36 | convolution fusion | flops 12885164032 | bytes 17825792 | tf_op jit(solution)/shard_map/fn,bfc->bnc/dot_general | solution.py:159
  277.3 2.4 copy.48
  279.8 6.8 %all-gather.6.cloned.1.call-done = bf16[8192,256]{1,0:T(8,128)(2,1)} async-done(((bf16[512,256]{1,0:T(8,128)(2,1)}), bf16[8192,256]{1,0:T(8,128)(2,1)}) %all-gather.6.cloned.1.call-update) | async-done | bytes 4194320 | tf_op jit(solution)/shard_map/all_gather | solution.py:106
  286.6 37.5 %while.30 = (s32[]{:T(128)}, f32[512,256]{1,0:T(8,128)S(1)}, s32[]{:T(128)}, bf16[16,512,256]{2,1,0:T(8,128)(2,1)}, bf16[8192,256]{1,0:T(8,128)(2,1)}, /*index=5...) while((s32[]{:T(128)}, f32[512,256]{1,0:T(8,128)S(1)}, s32[]{:T(128)}, ...), condition=%wide.region_1.2_spmd.clone, body=%wide.region_0.1_spmd.clone.sunk | while | flops 1310987 | bytes 4719323 | solution.py:116
  327.0 10.7 %collective-permute-done.1 = bf16[2,768]{0,1:T(8,128)(2,1)S(1)} collective-permute-done((bf16[2,768]{0,1:T(8,128)(2,1)S(1)}, bf16[2,768]{0,1:T(8,128)(2,1)S(1)}, u32[]{:S(2)}, u32[]{:S(2)}) %collective-permute-start.1) | collective-permute-done | bytes 3104 | tf_op jit(solution)/shard_map/ppermute | solution.py:11
  340.0 28.7 %reduce-scatter.2.cloned.1.call-done = bf16[256,256]{1,0:T(8,128)(2,1)} async-done(((bf16[4096,256]{1,0:T(8,128)(2,1)}), bf16[256,256]{1,0:T(8,128)(2,1)}) %reduce-scatter.2.cloned.1.call-update) | async-done | bytes 131088 | tf_op jit(solution)/shard_map/reduce_scatter | solution.py:163
  (257 shorter events, 116.5 us)
Async XLA Ops:
  7.2 56.6 %all-gather.4.cloned.1.call-start = ((), (), s32[]{:S(2)}) async-start(), calls=%async_computation.1 | async-start | bytes 2228224 | tf_op jit(solution)/shard_map/all_gather | solution.py:79
  7.9 8.8 %copy-start.8 = (f32[3,3,256]{2,1,0:T(4,128)S(1)}, f32[3,3,256]{2,1,0:T(4,128)}, u32[]{:S(2)}) copy-start(f32[3,3,256]{2,1,0:T(4,128)} %param.11) | copy-start | bytes 27652
  7.9 177.5 %all-gather.8.cloned.1.call-start = ((), (), s32[]{:S(2)}) async-start(), calls=%async_computation.3 | async-start | bytes 4456448 | tf_op jit(solution)/shard_map/all_gather | solution.py:136
  18.9 62.0 %copy-start.5 = (bf16[256,256]{1,0:T(8,128)(2,1)}, bf16[256,256]{1,0:T(8,128)(2,1)S(1)}, u32[]{:S(2)}) copy-start(bf16[256,256]{1,0:T(8,128)(2,1)S(1)} %select_convert_fusion) | copy-start | bytes 393220
  69.0 5.3 %collective-permute-start = (bf16[2,768]{1,0:T(2,128)(2,1)S(1)}, bf16[2,768]{1,0:T(2,128)(2,1)S(1)}, u32[]{:S(2)}, u32[]{:S(2)}) collective-permute-start(bf16[2,768]{1,0:T(2,128)(2,1)S(1)} %slice.215), channel_id=1, source_target_pairs={{0,16},{16,32},{32,48},{48,64},{64,80},{80,96},{96,112},{112,128},... | collective-permute-start | bytes 9224 | tf_op jit(solution)/shard_map/ppermute | solution.py:11
  76.3 4.6 %copy-start.7 = (bf16[256,256]{1,0:T(8,128)(2,1)S(1)}, bf16[256,256]{1,0:T(8,128)(2,1)}, u32[]{:S(2)}) copy-start(bf16[256,256]{1,0:T(8,128)(2,1)} %param.13) | copy-start | bytes 393220
  79.0 3.0 slice-start
  80.9 1.1 copy-start.1
  81.9 204.6 %all-gather.6.cloned.1.call-start = ((), (), s32[]{:S(2)}) async-start(), calls=%async_computation.2 | async-start | bytes 4456448 | tf_op jit(solution)/shard_map/all_gather | solution.py:106
  90.4 13.1 %copy-start.3 = (bf16[512,512]{1,0:T(8,128)(2,1)}, bf16[512,512]{1,0:T(8,128)(2,1)S(1)}, u32[]{:S(2)}) copy-start(bf16[512,512]{1,0:T(8,128)(2,1)S(1)} %fusion.20) | copy-start | bytes 1572868
  105.5 84.1 %copy-start = (bf16[512,256]{1,0:T(8,128)(2,1)S(1)}, bf16[512,256]{1,0:T(8,128)(2,1)}, u32[]{:S(2)}) copy-start(bf16[512,256]{1,0:T(8,128)(2,1)} %convolution_convert_fusion.2) | copy-start | bytes 786436
  105.5 263.3 %reduce-scatter.2.cloned.1.call-start = ((), (), s32[]{:S(2)}) async-start(), calls=%async_computation.4 | async-start | bytes 2228224 | tf_op jit(solution)/shard_map/reduce_scatter | solution.py:163
  286.6 37.5 %copy-start.2 = (f32[256,3,256]{2,0,1:T(8,128)S(1)}, f32[256,3,256]{2,0,1:T(8,128)}, u32[]{:S(2)}) copy-start(f32[256,3,256]{2,0,1:T(8,128)} %copy-done.1) | copy-start | bytes 2359300
  286.6 37.5 %copy-start.4 = (bf16[512,512]{1,0:T(8,128)(2,1)S(1)}, bf16[512,512]{1,0:T(8,128)(2,1)}, u32[]{:S(2)}) copy-start(bf16[512,512]{1,0:T(8,128)(2,1)} %copy-done.3) | copy-start | bytes 1572868
  286.6 37.8 %copy-start.6 = (bf16[256,256]{1,0:T(8,128)(2,1)S(1)}, bf16[256,256]{1,0:T(8,128)(2,1)}, u32[]{:S(2)}) copy-start(bf16[256,256]{1,0:T(8,128)(2,1)} %copy-done.5) | copy-start | bytes 393220
  325.5 12.2 %collective-permute-start.1 = (bf16[2,768]{0,1:T(8,128)(2,1)S(1)}, bf16[2,768]{0,1:T(8,128)(2,1)S(1)}, u32[]{:S(2)}, u32[]{:S(2)}) collective-permute-start(bf16[2,768]{0,1:T(8,128)(2,1)S(1)} %copy.43), channel_id=1, source_target_pairs={{16,0},{32,16},{48,32},{64,48},{80,64},{96,80},{112,96},{128,112},... | collective-permute-start | bytes 9224 | tf_op jit(solution)/shard_map/ppermute | solution.py:11
Sparse Core Ops, SparseCore 0:
  10.5 53.1 all-gather.3
  82.0 103.3 all-gather.7
  187.8 98.7 all-gather.5
  288.9 79.7 reduce-scatter.1
where the time goes:
time: 380 us; the launch traced here: 377 us
  waiting for transfers between devices  173 us (46%)
  other arithmetic  116 us (31%)
  local copies, waits for them, and re-layouts  34.6 us (9%)
  matrix products  32.6 us (9%)
  between operations  14.1 us (4%)
  starting transfers between devices  5.63 us (1%)
    all_gather x1, waiting for transfers between devices, on_device(): backward_pieces = lax.all_gather(grad_spec, 'seq', axis=0, tiled=True)  79.7 us
    all_gather x1, waiting for transfers between devices, on_device(): lax.all_gather(tokens, 'chan', axis=1, tiled=True)  44.9 us
    dynamic_update_slice x16, other arithmetic, backward_add_block(): lax.dynamic_update_index_in_dim(filter_grad, current, clipped, 0)  30.7 us
    reduce_scatter x1, waiting for transfers between devices, on_device(): lax.psum_scatter(tap_terms.reshape(seq_count * row_count, local_width).as...  28.7 us
    dot_general x1, matrix products, on_device(): jnp.einsum('fn,bfc->bnc', forward, filter_grad, precision=lax.Precision.H...  16.5 us
    convert_element_type x32, other arithmetic, spectral_adjoint(): left_spec = left_spec.astype(jnp.float32)  16.5 us
    convert_element_type x16, other arithmetic, spectral_product(): right_spec = right_spec.astype(jnp.float32)  16 us
    convert_element_type x16, other arithmetic, spectral_product(): left_spec = left_spec.astype(jnp.float32)  15.9 us
  transfers between devices with their start and end apart: 6, of which 6 were waited for; matrix products, arithmetic and copies ran while one was open for 45% of the time, Pallas kernels for 0%

commit v1 on v0

--- a/solution.py
+++ b/solution.py
@@ -133,7 +133,9 @@
         jnp.zeros((spec_rows, local_width), jnp.float32),
         jnp.zeros((seq_count, spec_rows, local_width), jnp.float32),
     )
-    backward_pieces = lax.all_gather(grad_spec, "seq", axis=0, tiled=True)
+    backward_pieces = jnp.concatenate(
+        lax.all_to_all(jnp.stack([grad_spec] * lax.axis_size("seq")), "seq", 0, 0), axis=0
+    )
 
     def backward_add_block(position, state):
         spectral_grad, filter_grad = state

time: 380 us -> 400 us (1.053)
  waiting for transfers between devices: 173 us -> 184 us
  starting transfers between devices: 5.63 us -> 15.4 us
    all_gather x1 -> x0, waiting for transfers between devices: 79.7 us -> none  [on_device(): backward_pieces = lax.all_gather(grad_spec, 'seq', axis=0, tiled=True)]
    all_to_all x0 -> x1, waiting for transfers between devices: none -> 76.4 us  [on_device(): lax.all_to_all(jnp.stack([grad_spec] * lax.axis_size('seq')), 'seq', 0, 0)]
    reduce_scatter x1, waiting for transfers between devices: 28.7 us -> 40.5 us  [on_device(): lax.psum_scatter(tap_terms.reshape(seq_count * row_count, local_width).as...]
    ppermute x2, waiting for transfers between devices: 12 us -> 21.6 us  [passed_along(): return lax.ppermute(block, axis, route)]
    all_to_all x0 -> x1, starting transfers between devices: none -> 9.6 us  [on_device(): lax.all_to_all(jnp.stack([grad_spec] * lax.axis_size('seq')), 'seq', 0, 0)]
    all_gather x1, waiting for transfers between devices: 6.8 us -> 0.02 us  [on_device(): pieces = lax.all_gather(own_spec, 'seq', axis=0, tiled=True)]
  transfers between devices with their start and end apart: 6 -> 6, of which waited for: 6 -> 5; matrix products, arithmetic and copies ran while one was open for 45% -> 43% of each run, Pallas kernels for 0% -> 0%
where the time goes in v1:
time: 400 us; the launch traced here: 396 us
  waiting for transfers between devices  184 us (46%)
  other arithmetic  114 us (28%)
  local copies, waits for them, and re-layouts  34.2 us (9%)
  matrix products  33 us (8%)
  starting transfers between devices  15.4 us (4%)
  between operations  14.2 us (4%)
    all_to_all x1, waiting for transfers between devices, on_device(): lax.all_to_all(jnp.stack([grad_spec] * lax.axis_size('seq')), 'seq', 0, 0)  76.4 us
    all_gather x1, waiting for transfers between devices, on_device(): lax.all_gather(tokens, 'chan', axis=1, tiled=True)  44.9 us
    reduce_scatter x1, waiting for transfers between devices, on_device(): lax.psum_scatter(tap_terms.reshape(seq_count * row_count, local_width).as...  40.5 us
    dynamic_update_slice x16, other arithmetic, backward_add_block(): lax.dynamic_update_index_in_dim(filter_grad, current, clipped, 0)  30.8 us
    ppermute x2, waiting for transfers between devices, passed_along(): return lax.ppermute(block, axis, route)  21.6 us
    dot_general x1, matrix products, on_device(): jnp.einsum('fn,bfc->bnc', forward, filter_grad, precision=lax.Precision.H...  16.5 us
    convert_element_type x32, other arithmetic, spectral_adjoint(): left_spec = left_spec.astype(jnp.float32)  16.5 us
    convert_element_type x16, other arithmetic, spectral_product(): right_spec = right_spec.astype(jnp.float32)  16 us
  transfers between devices with their start and end apart: 6, of which 5 were waited for; matrix products, arithmetic and copies ran while one was open for 43% of the time, Pallas kernels for 0%

profile of v1, /device:TPU:20, one launch (start us, length us, event | category | flops | bytes accessed | tf_op | source)
XLA Modules:
  0.0 396.5 jit_solution(13066291833006537460)
XLA Ops:
  7.9 8.7 %copy.31 = bf16[4096,3,256]{0,2,1:T(8,128)(2,1)} copy(bf16[4096,3,256]{2,0,1:T(8,128)(2,1)} %param.10) | data formatting | bytes 12582912 | tf_op args[1]
  18.9 44.9 %all-gather.3.cloned.1.call-done = bf16[256,4096]{1,0:T(8,128)(2,1)} async-done(((bf16[256,256]{1,0:T(8,128)(2,1)}), bf16[256,4096]{1,0:T(8,128)(2,1)}) %all-gather.3.cloned.1.call-update) | async-done | bytes 2097168 | tf_op jit(solution)/shard_map/all_gather | solution.py:79
  63.8 5.2 %convolution_convert_fusion = bf16[256,768]{1,0:T(8,128)(2,1)S(1)} fusion(bf16[256,4096]{1,0:T(8,128)(2,1)} %all-gather.3.cloned.1.call-done, bf16[4096,768]{0,1:T(8,128)(2,1)} %bitcast.105), kind=kOutput, calls=%fused_computation.38 | convolution fusion | flops 1610809344 | bytes 8781824 | tf_op jit(solution)/shard_map/dot_general | solution.py:78
  69.0 4.0 %collective-permute-start = (bf16[2,768]{1,0:T(2,128)(2,1)S(1)}, bf16[2,768]{1,0:T(2,128)(2,1)S(1)}, u32[]{:S(2)}, u32[]{:S(2)}) collective-permute-start(bf16[2,768]{1,0:T(2,128)(2,1)S(1)} %slice.215), channel_id=1, source_target_pairs={{0,16},{16,32},{32,48},{48,64},{64,80},{80,96},{96,112},{112,128},... | collective-permute-start | bytes 9224 | tf_op jit(solution)/shard_map/ppermute | solution.py:11
  77.7 2.4 stack.11
  80.1 9.6 %all-to-all-start = ((bf16[16,512,256]{2,1,0:T(8,128)(2,1)}), bf16[16,512,256]{2,1,0:T(8,128)(2,1)}, u32[]{:S(2)}, u32[]{:S(2)}) async-start(bf16[16,512,256]{2,1,0:T(8,128)(2,1)} %stack.11), calls=%async_computation | async-start | bytes 8388608 | tf_op jit(solution)/shard_map/all_to_all | solution.py:137
  90.0 2.3 copy.38
  92.3 3.9 copy.39
  96.2 2.1 negate_select_fusion.2
  98.5 6.8 %convert_bitcast_fusion = bf16[16,512,256]{1,2,0:T(8,128)(2,1)} fusion(bf16[15,256,256]{1,2,0:T(8,128)(2,1)} %copy.38, bf16[16,256,256]{1,2,0:T(8,128)(2,1)} %copy.39, bf16[512,512]{1,0:T(8,128)(2,1)S(1)} %fusion.20), kind=kOutput, calls=%fused_computation.35 | convolution fusion | flops 2162163712 | bytes 8781824 | tf_op jit(solution)/shard_map/fn,bnc->bfc/dot_general | solution.py:103
  105.2 6.4 %copy.40 = bf16[16,512,256]{2,1,0:T(8,128)(2,1)} copy(bf16[16,512,256]{1,2,0:T(8,128)(2,1)} %convert_bitcast_fusion) | data formatting | bytes 8388608
  111.6 2.0 convolution_convert_fusion.2
  113.9 76.4 %all-to-all-done = bf16[16,512,256]{2,1,0:T(8,128)(2,1)} async-done(((bf16[16,512,256]{2,1,0:T(8,128)(2,1)}), bf16[16,512,256]{2,1,0:T(8,128)(2,1)}, u32[]{:S(2)}, u32[]{:S(2)}) %all-to-all-start) | async-done | bytes 4194336 | tf_op jit(solution)/shard_map/all_to_all | solution.py:137
  190.2 4.1 %broadcast_in_dim.154 = f32[16,512,256]{2,1,0:T(8,128)} broadcast(f32[]{:T(128)} %constant.182.clone.1), dimensions={} | broadcast | bytes 8388612 | tf_op jit(solution)/shard_map/broadcast_in_dim | solution.py:134
  194.4 69.8 %while.31 = (s32[]{:T(128)}, f32[512,256]{1,0:T(8,128)S(1)}, f32[16,512,256]{2,1,0:T(8,128)}, s32[]{:T(128)}, bf16[16,512,256]{2,1,0:T(8,128)(2,1)}, /*index=5*/...) while((s32[]{:T(128)}, f32[512,256]{1,0:T(8,128)S(1)}, ...), condition=%wide.region_3.4_spmd.clone, body=%wide.region_2.3_spmd.clone.sunk | while | flops 2359563 | bytes 8127216 | solution.py:155
  201.2 1.9 fusion.74
  249.1 1.9 fusion.74
  257.8 1.9 fusion.74
  262.2 2.0 fusion.74
  264.2 16.5 %convolution_bitcast_fusion = f32[16,512,256]{1,2,0:T(8,128)S(1)} fusion(f32[16,512,256]{2,1,0:T(8,128)} %get-tuple-element.224, f32[256,512]{1,0:T(8,128)S(1)} %get-tuple-element.350, f32[256,512]{1,0:T(8,128)S(1)} %get-tuple-element.351), kind=kOutput, calls=%fused_computation.36 | convolution fusion | flops 12885164032 | bytes 17825792 | tf_op jit(solution)/shard_map/fn,bfc->bnc/dot_general | solution.py:161
  282.2 2.4 copy.48
  284.7 37.5 %while.30 = (s32[]{:T(128)}, f32[512,256]{1,0:T(8,128)S(1)}, s32[]{:T(128)}, bf16[16,512,256]{2,1,0:T(8,128)(2,1)}, bf16[8192,256]{1,0:T(8,128)(2,1)}, /*index=5...) while((s32[]{:T(128)}, f32[512,256]{1,0:T(8,128)S(1)}, s32[]{:T(128)}, ...), condition=%wide.region_1.2_spmd.clone, body=%wide.region_0.1_spmd.clone.sunk | while | flops 1310987 | bytes 4719323 | solution.py:116
  325.1 20.4 %collective-permute-done.1 = bf16[2,768]{0,1:T(8,128)(2,1)S(1)} collective-permute-done((bf16[2,768]{0,1:T(8,128)(2,1)S(1)}, bf16[2,768]{0,1:T(8,128)(2,1)S(1)}, u32[]{:S(2)}, u32[]{:S(2)}) %collective-permute-start.1) | collective-permute-done | bytes 3104 | tf_op jit(solution)/shard_map/ppermute | solution.py:11
  347.8 40.5 %reduce-scatter.2.cloned.1.call-done = bf16[256,256]{1,0:T(8,128)(2,1)} async-done(((bf16[4096,256]{1,0:T(8,128)(2,1)}), bf16[256,256]{1,0:T(8,128)(2,1)}) %reduce-scatter.2.cloned.1.call-update) | async-done | bytes 131088 | tf_op jit(solution)/shard_map/reduce_scatter | solution.py:165
  (257 shorter events, 114.5 us)
Async XLA Ops:
  7.2 56.6 %all-gather.3.cloned.1.call-start = ((), (), s32[]{:S(2)}) async-start(), calls=%async_computation.2 | async-start | bytes 2228224 | tf_op jit(solution)/shard_map/all_gather | solution.py:79
  7.9 8.8 %copy-start.8 = (f32[3,3,256]{2,1,0:T(4,128)S(1)}, f32[3,3,256]{2,1,0:T(4,128)}, u32[]{:S(2)}) copy-start(f32[3,3,256]{2,1,0:T(4,128)} %param.11) | copy-start | bytes 27652
  18.8 57.5 %copy-start.5 = (bf16[256,256]{1,0:T(8,128)(2,1)}, bf16[256,256]{1,0:T(8,128)(2,1)S(1)}, u32[]{:S(2)}) copy-start(bf16[256,256]{1,0:T(8,128)(2,1)S(1)} %select_convert_fusion) | copy-start | bytes 393220
  69.0 5.3 %collective-permute-start = (bf16[2,768]{1,0:T(2,128)(2,1)S(1)}, bf16[2,768]{1,0:T(2,128)(2,1)S(1)}, u32[]{:S(2)}, u32[]{:S(2)}) collective-permute-start(bf16[2,768]{1,0:T(2,128)(2,1)S(1)} %slice.215), channel_id=1, source_target_pairs={{0,16},{16,32},{32,48},{48,64},{64,80},{80,96},{96,112},{112,128},... | collective-permute-start | bytes 9224 | tf_op jit(solution)/shard_map/ppermute | solution.py:11
  76.4 3.7 copy-start.1
  80.1 9.9 %slice-start = ((bf16[4096,256]{1,0:T(8,128)(2,1)}), bf16[3840,256]{1,0:T(8,128)(2,1)S(1)}, s32[]{:S(2)}) async-start(bf16[4096,256]{1,0:T(8,128)(2,1)} %param.12), calls=%async_computation.5 | async-start | bytes 3932160 | tf_op jit(solution)/shard_map/slice | solution.py:100
  80.1 110.1 %all-to-all-start = ((bf16[16,512,256]{2,1,0:T(8,128)(2,1)}), bf16[16,512,256]{2,1,0:T(8,128)(2,1)}, u32[]{:S(2)}, u32[]{:S(2)}) async-start(bf16[16,512,256]{2,1,0:T(8,128)(2,1)} %stack.11), calls=%async_computation | async-start | bytes 8388608 | tf_op jit(solution)/shard_map/all_to_all | solution.py:137
  89.7 194.9 %all-gather.5.cloned.1.call-start = ((), (), s32[]{:S(2)}) async-start(), calls=%async_computation.3 | async-start | bytes 4456448 | tf_op jit(solution)/shard_map/all_gather | solution.py:106
  98.4 13.2 %copy-start.3 = (bf16[512,512]{1,0:T(8,128)(2,1)}, bf16[512,512]{1,0:T(8,128)(2,1)S(1)}, u32[]{:S(2)}) copy-start(bf16[512,512]{1,0:T(8,128)(2,1)S(1)} %fusion.20) | copy-start | bytes 1572868
  113.6 274.7 %reduce-scatter.2.cloned.1.call-start = ((), (), s32[]{:S(2)}) async-start(), calls=%async_computation.4 | async-start | bytes 2228224 | tf_op jit(solution)/shard_map/reduce_scatter | solution.py:165
  190.2 4.1 %copy-start = (bf16[512,256]{1,0:T(8,128)(2,1)S(1)}, bf16[512,256]{1,0:T(8,128)(2,1)}, u32[]{:S(2)}) copy-start(bf16[512,256]{1,0:T(8,128)(2,1)} %convolution_convert_fusion.2) | copy-start | bytes 786436
  284.6 37.5 %copy-start.2 = (f32[256,3,256]{2,0,1:T(8,128)S(1)}, f32[256,3,256]{2,0,1:T(8,128)}, u32[]{:S(2)}) copy-start(f32[256,3,256]{2,0,1:T(8,128)} %copy-done.1) | copy-start | bytes 2359300
  284.6 37.5 %copy-start.4 = (bf16[512,512]{1,0:T(8,128)(2,1)S(1)}, bf16[512,512]{1,0:T(8,128)(2,1)}, u32[]{:S(2)}) copy-start(bf16[512,512]{1,0:T(8,128)(2,1)} %copy-done.3) | copy-start | bytes 1572868
  284.6 37.8 %copy-start.6 = (bf16[256,256]{1,0:T(8,128)(2,1)S(1)}, bf16[256,256]{1,0:T(8,128)(2,1)}, u32[]{:S(2)}) copy-start(bf16[256,256]{1,0:T(8,128)(2,1)} %copy-done.5) | copy-start | bytes 393220
  284.6 38.7 %copy-start.7 = (bf16[256,256]{1,0:T(8,128)(2,1)S(1)}, bf16[256,256]{1,0:T(8,128)(2,1)}, u32[]{:S(2)}) copy-start(bf16[256,256]{1,0:T(8,128)(2,1)} %param.13) | copy-start | bytes 393220
  323.6 21.8 %collective-permute-start.1 = (bf16[2,768]{0,1:T(8,128)(2,1)S(1)}, bf16[2,768]{0,1:T(8,128)(2,1)S(1)}, u32[]{:S(2)}, u32[]{:S(2)}) collective-permute-start(bf16[2,768]{0,1:T(8,128)(2,1)S(1)} %copy.43), channel_id=1, source_target_pairs={{16,0},{32,16},{48,32},{64,48},{80,64},{96,80},{112,96},{128,112},... | collective-permute-start | bytes 9224 | tf_op jit(solution)/shard_map/ppermute | solution.py:11
Sparse Core Ops, SparseCore 0:
  10.5 53.1 all-gather.2
  113.7 149.1 all-gather.4
  284.7 103.5 reduce-scatter.1
